TPU v7x, 256 devices: a whole 4x4x8 slice. The times are simulated.
256 devices in a mesh: tm: 8 (over y_lo, x), stn: 32 (over y_hi, z, core).
Axes of the slice: x: 4, y: 4 (y_hi: 2, y_lo: 2; y = y_hi * 2 + y_lo), z: 8, core: 2. Of those that a mesh axis runs over, the one named last changes fastest.
Arguments:
- voltages: bfloat16 [1024, 524288], P('stn', 'tm'), may hold values from -6 to 6
- gains: float32 [2, 1024, 256], P(None, 'stn'), may hold values from -4 to 4
Outputs:
- visibility: float32 [256, 2, 1024, 1024], P(('tm', 'stn'))
All inputs are finite; a program needn't handle non-finite values.
Results may differ from a plain program's by a relative error of at most 0.0038.
Values may be sent and summed in bfloat16 or wider, within the bound.
No kernel may reach another device: no remote copies, remote signals or barrier semaphores. Data moves between devices by JAX's collectives and lax.ppermute only.
A program may use at most 128 MiB of HBM per device.

v0:
```python
import jax
import jax.numpy as jnp
from jax import lax
from jax.sharding import PartitionSpec as P

CHANNELS = 4096
BAND_LOW = 1024
TAPS = 8


def passed_along(x, axis, by):
    devices = lax.axis_size(axis)
    pairs = [(i, i + by) for i in range(devices) if 0 <= i + by < devices]
    return lax.ppermute(x, axis, pairs)


def window_table(chans):
    frame_len = 2 * chans
    total_len = TAPS * frame_len
    positions = jnp.arange(total_len, dtype=jnp.float32)
    centred = (positions - (total_len - 1) / 2.0) / frame_len
    taper = jnp.sin(jnp.pi * (positions + 0.5) / total_len)
    shaped = jnp.sinc(centred) * taper * taper
    shaped = shaped / jnp.sqrt(jnp.sum(shaped * shaped))
    return shaped.reshape(TAPS, frame_len)


def band_tables(frame_len, band):
    sample_index = jnp.arange(frame_len, dtype=jnp.int32)[:, None]
    channel_index = (BAND_LOW + jnp.arange(band, dtype=jnp.int32))[None, :]
    phase = (sample_index * channel_index % frame_len).astype(jnp.float32)
    angles = 2.0 * jnp.pi * phase / frame_len
    return (jnp.cos(angles), jnp.sin(angles))


def band_spectra(windowed, cos_table, sin_table):
    highest = lax.Precision.HIGHEST
    real_part = jnp.einsum("ifm,mk->kif", windowed, cos_table, precision=highest)
    imag_part = -jnp.einsum("ifm,mk->kif", windowed, sin_table, precision=highest)
    return (real_part, imag_part)


def apply_taps(window, extended, frames):
    windowed = jnp.zeros((extended.shape[0], frames, extended.shape[2]), jnp.float32)
    for tap_index in range(TAPS):
        windowed = windowed + window[tap_index] * extended[
            :, tap_index : tap_index + frames, :
        ].astype(jnp.float32)
    return windowed


def operands(turned):
    stacked = jnp.concatenate([turned[0], turned[1]], axis=-1)
    flipped = jnp.concatenate([turned[1], -turned[0]], axis=-1)
    return (stacked, flipped)


def cross_power(stacked, flipped, total_frames):
    vis_real = jnp.einsum("cif,cjf->cij", stacked, stacked, preferred_element_type=jnp.float32)
    vis_imag = jnp.einsum("cif,cjf->cij", flipped, stacked, preferred_element_type=jnp.float32)
    return jnp.stack([vis_real, vis_imag], axis=1) / total_frames


def on_device(voltages, gains):
    in_dev, length = voltages.shape
    band = gains.shape[2]
    frame_len = 2 * CHANNELS
    frames = length // frame_len
    n_time = lax.axis_size("tm")
    n_station = lax.axis_size("stn")
    per_device = band // (n_time * n_station)
    all_inputs = in_dev * n_station
    history = TAPS - 1
    window = window_table(CHANNELS)
    cos_table, sin_table = band_tables(frame_len, band)
    framed = voltages.reshape(in_dev, frames, frame_len)
    before = passed_along(framed[:, frames - history :, :], "tm", 1)
    extended = jnp.concatenate([before, framed], axis=1)
    windowed = apply_taps(window, extended, frames)
    raw_real, raw_imag = band_spectra(windowed, cos_table, sin_table)
    gain_real = jnp.transpose(gains[0])[:, :, None]
    gain_imag = jnp.transpose(gains[1])[:, :, None]
    spec_real = gain_real * raw_real - gain_imag * raw_imag
    spec_imag = gain_real * raw_imag + gain_imag * raw_real
    spectra = jnp.stack([spec_real, spec_imag]).astype(jnp.bfloat16)
    blocks = spectra.reshape(2, n_time, n_station, per_device, in_dev, frames)
    turned = lax.all_to_all(
        lax.all_to_all(blocks, "tm", split_axis=1, concat_axis=5, tiled=True),
        "stn",
        split_axis=2,
        concat_axis=4,
        tiled=True,
    )
    turned = turned.reshape(2, per_device, all_inputs, n_time * frames)
    stacked, flipped = operands(turned)
    return cross_power(stacked, flipped, float(n_time * frames))


def solution(mesh):
    in_specs = (P("stn", "tm"), P(None, "stn", None))
    out_specs = P(("tm", "stn"), None, None, None)
    return jax.shard_map(
        on_device, mesh=mesh, in_specs=in_specs, out_specs=out_specs, check_vma=False
    )
```

profile of v0, /device:TPU:1, one launch (start us, length us, event | category | flops | bytes accessed | tf_op | source)
XLA Modules:
  0.0 223.4 jit_solution(14158245446705456912)
XLA Ops:
  0.0 0.0 copy-start.1
  0.0 2.5 %copy.34 = bf16[4,8,8,8192]{3,2,0,1:T(8,128)(2,1)S(1)} copy(bf16[4,8,8,8192]{3,2,1,0:T(8,128)(2,1)} %bitcast.57) | data formatting | bytes 8388608 | tf_op jit(solution)/shard_map/reshape | solution.py:76
  2.5 2.1 slice.94
  4.6 5.7 %collective-permute-start = (bf16[32,7,8192]{2,0,1:T(8,128)(2,1)}, bf16[32,7,8192]{2,0,1:T(8,128)(2,1)}, u32[]{:S(2)}, u32[]{:S(2)}) collective-permute-start(bf16[32,7,8192]{2,0,1:T(8,128)(2,1)} %slice.94), channel_id=1, source_target_pairs={{0,32},{32,64},{64,96},{96,128},{128,160},{160,192},{192,224},{1,3... | collective-permute-start | bytes 11010056 | tf_op jit(solution)/shard_map/ppermute | solution.py:14
  10.3 1.9 multiply_reduce_fusion
  13.0 0.0 copy-start
  13.0 0.0 copy-done.1
  13.0 1.2 broadcast_divide_fusion
  14.3 72.5 %collective-permute-done = bf16[32,7,8192]{2,0,1:T(8,128)(2,1)} collective-permute-done((bf16[32,7,8192]{2,0,1:T(8,128)(2,1)}, bf16[32,7,8192]{2,0,1:T(8,128)(2,1)}, u32[]{:S(2)}, u32[]{:S(2)}) %collective-permute-start) | collective-permute-done | bytes 3670048 | tf_op jit(solution)/shard_map/ppermute | solution.py:14
  86.8 2.3 %constant_dynamic-update-slice_fusion.1 = bf16[32,15,8192]{2,0,1:T(8,128)(2,1)S(1)} fusion(bf16[32,7,8192]{2,0,1:T(8,128)(2,1)} %collective-permute-done), kind=kLoop, calls=%fused_computation.69 | loop fusion | bytes 7340032
  89.1 0.0 copy-done
  89.1 0.4 constant_dynamic-update-slice_fusion
  89.6 7.9 %multiply_add_fusion = f32[32,8,8192]{2,0,1:T(8,128)S(1)} fusion(bf16[32,15,8192]{2,0,1:T(8,128)(2,1)S(1)} %constant_dynamic-update-slice_fusion, f32[8192]{0:T(1024)S(1)} %get-tuple-element.10, f32[8192]{0:T(1024)S(1)} %get-tuple-element.11, f32[8192]{0:T(1024)S(1)} %get-tuple-element.12, f32[8192]{0:T(1024)S(1)} %get-tuple-element.13, ...), kind=kLoop, calls=%fused_computation.12 | loop fusion | flops 48234496 | bytes 42205184 | tf_op jit(solution)/shard_map/add | solution.py:46
  97.5 38.5 %fusion.5 = f32[256,32,8]{0,1,2:T(8,128)S(1)} fusion(f32[32,8,8192]{2,0,1:T(8,128)S(1)} %multiply_add_fusion, s32[256]{0:T(256)S(1)} %iota_add_fusion.2), kind=kOutput, calls=%fused_computation.9 | convolution fusion | flops 6471811072 | bytes 8651776 | tf_op jit(solution)/shard_map/ifm,mk->kif/dot_general | solution.py:38
  136.0 38.8 %subtract_convert_fusion = (bf16[256,32,8]{0,1,2:T(8,128)(2,1)S(1)}, bf16[256,32,8]{0,1,2:T(8,128)(2,1)S(1)}) fusion(f32[256,32,8]{0,1,2:T(8,128)S(1)} %fusion.5, f32[256,32]{0,1:T(8,128)S(1)} %get-tuple-element.18, f32[256,32]{0,1:T(8,128)S(1)} %get-tuple-element.17, f32[32,8,8192]{2,0,1:T(8,128)S(1)} %multiply_add_fusion, s32[256]{0:T(256)S(1)} %iota_add_fusion.2), kind=kOutput, calls=%fused_computation.63 | convolution fusion | flops 6472400896 | bytes 8979456 | tf_op jit(solution)/shard_map/ifm,mk->kif/dot_general | solution.py:39
  174.8 0.3 copy.25
  175.1 0.3 copy.26
  175.4 0.2 fusion.57
  175.6 1.0 reshape.144
  176.6 12.0 %all_to_all.27 = bf16[8,2,8192]{2,1,0:T(2,128)(2,1)S(1)} all-to-all(bf16[8,2,8192]{2,1,0:T(2,128)(2,1)S(1)} %reshape.144), channel_id=1, replica_groups=mesh['tm'=8,'stn'=32] {'tm'}, dimensions={0} | all-to-all | bytes 524288 | tf_op jit(solution)/shard_map/all_to_all | solution.py:88
  188.5 0.5 reshape.145
  189.0 0.3 copy_bitcast_fusion.1
  189.3 0.4 copy.24
  189.7 0.4 reshape.146
  190.1 26.8 %all_to_all.28 = bf16[32,2,2048]{2,1,0:T(2,128)(2,1)S(1)} all-to-all(bf16[32,2,2048]{2,1,0:T(2,128)(2,1)S(1)} %reshape.146), channel_id=1, replica_groups=mesh['tm'=8,'stn'=32] {'stn'}, dimensions={0} | all-to-all | bytes 524288 | tf_op jit(solution)/shard_map/all_to_all | solution.py:87
  216.9 0.4 reshape.147
  217.3 0.1 neg.22
  217.3 0.8 convolution_bitcast_fusion.1
  218.2 0.8 convolution_bitcast_fusion
  219.0 4.4 %maximum_multiply_fusion = f32[1,2,1024,1024]{3,2,1,0:T(8,128)} fusion(f32[1,1,1024,1024]{3,2,1,0:T(8,128)S(1)} %convolution_bitcast_fusion, f32[1,1,1024,1024]{3,2,1,0:T(8,128)S(1)} %convolution_bitcast_fusion.1), kind=kLoop, calls=%fused_computation.6 | loop fusion | flops 4194304 | bytes 16777216 | tf_op jit(solution)/shard_map/div | solution.py:61
  (4 shorter events, 0.1 us)
Async XLA Ops:
  0.0 13.0 %copy-start.1 = (f32[2,32,256]{2,1,0:T(8,128)S(1)}, f32[2,32,256]{2,1,0:T(8,128)}, u32[]{:S(2)}) copy-start(f32[2,32,256]{2,1,0:T(8,128)} %param.3) | copy-start | bytes 196612
  4.6 82.2 %collective-permute-start = (bf16[32,7,8192]{2,0,1:T(8,128)(2,1)}, bf16[32,7,8192]{2,0,1:T(8,128)(2,1)}, u32[]{:S(2)}, u32[]{:S(2)}) collective-permute-start(bf16[32,7,8192]{2,0,1:T(8,128)(2,1)} %slice.94), channel_id=1, source_target_pairs={{0,32},{32,64},{64,96},{96,128},{128,160},{160,192},{192,224},{1,3... | collective-permute-start | bytes 11010056 | tf_op jit(solution)/shard_map/ppermute | solution.py:14
  13.0 76.1 %copy-start = (bf16[32,65536]{1,0:T(8,128)(2,1)S(1)}, bf16[32,65536]{1,0:T(8,128)(2,1)}, u32[]{:S(2)}) copy-start(bf16[32,65536]{1,0:T(8,128)(2,1)} %param.2) | copy-start | bytes 12582916
where the time goes:
time: 224 us; the launch traced here: 223 us
  matrix products  78.9 us (35%)
  waiting for transfers between devices  72.5 us (32%)
  blocking collectives  38.7 us (17%)
  other arithmetic  15.7 us (7%)
  local copies, waits for them, and re-layouts  10.8 us (5%)
  starting transfers between devices  5.72 us (3%)
    ppermute x1, waiting for transfers between devices, passed_along(): return lax.ppermute(x, axis, pairs)  72.5 us
    dot_general x1, matrix products, band_spectra(): jnp.einsum('ifm,mk->kif', windowed, sin_table, precision=highest)  38.8 us
    dot_general x1, matrix products, band_spectra(): jnp.einsum('ifm,mk->kif', windowed, cos_table, precision=highest)  38.5 us
    all_to_all x1, blocking collectives, on_device(): lax.all_to_all(lax.all_to_all(blocks, 'tm', split_axis=1, concat_axis=5,...  26.8 us
    all_to_all x1, blocking collectives, on_device(): lax.all_to_all(blocks, 'tm', split_axis=1, concat_axis=5, tiled=True)  12 us
    add x1, other arithmetic, apply_taps(): windowed + window[tap_index] * extended[:, tap_index:tap_index + frames,...  7.9 us
    ppermute x1, starting transfers between devices, passed_along(): return lax.ppermute(x, axis, pairs)  5.72 us
  transfers between devices with their start and end apart: 1, of which 1 were waited for; matrix products, arithmetic and copies ran while one was open for 1% of the time, Pallas kernels for 0%

commit v1 on v0

--- a/solution.py
+++ b/solution.py
@@ -62,6 +62,15 @@
 
 
 def on_device(voltages, gains):
+
+    def lift_pages_here(x_local, axis_id):
+        return jnp.concatenate(
+            lax.all_to_all(
+                jnp.stack(jnp.split(x_local, lax.axis_size(axis_id), 1), 0), axis_id, 0, 0
+            ),
+            5,
+        )
+
     in_dev, length = voltages.shape
     band = gains.shape[2]
     frame_len = 2 * CHANNELS
@@ -85,11 +94,7 @@
     spectra = jnp.stack([spec_real, spec_imag]).astype(jnp.bfloat16)
     blocks = spectra.reshape(2, n_time, n_station, per_device, in_dev, frames)
     turned = lax.all_to_all(
-        lax.all_to_all(blocks, "tm", split_axis=1, concat_axis=5, tiled=True),
-        "stn",
-        split_axis=2,
-        concat_axis=4,
-        tiled=True,
+        lift_pages_here(blocks, "tm"), "stn", split_axis=2, concat_axis=4, tiled=True
     )
     turned = turned.reshape(2, per_device, all_inputs, n_time * frames)
     stacked, flipped = operands(turned)

time: 224 us -> 224 us (level)
  no operation moved by 1% of the time
where the time goes in v1:
time: 224 us; the launch traced here: 223 us
  matrix products  78.9 us (35%)
  waiting for transfers between devices  72.5 us (32%)
  blocking collectives  38.7 us (17%)
  other arithmetic  15.9 us (7%)
  local copies, waits for them, and re-layouts  10.8 us (5%)
  starting transfers between devices  5.72 us (3%)
    ppermute x1, waiting for transfers between devices, passed_along(): return lax.ppermute(x, axis, pairs)  72.5 us
    dot_general x1, matrix products, band_spectra(): jnp.einsum('ifm,mk->kif', windowed, sin_table, precision=highest)  38.8 us
    dot_general x1, matrix products, band_spectra(): jnp.einsum('ifm,mk->kif', windowed, cos_table, precision=highest)  38.5 us
    all_to_all x1, blocking collectives, on_device(): lax.all_to_all(lift_pages_here(blocks, 'tm'), 'stn', split_axis=2, concat...  26.8 us
    all_to_all x1, blocking collectives, lift_pages_here(): lax.all_to_all(jnp.stack(jnp.split(x_local, lax.axis_size(axis_id), 1), 0...  12 us
    add x1, other arithmetic, apply_taps(): windowed + window[tap_index] * extended[:, tap_index:tap_index + frames,...  7.9 us
    ppermute x1, starting transfers between devices, passed_along(): return lax.ppermute(x, axis, pairs)  5.72 us
  transfers between devices with their start and end apart: 1, of which 1 were waited for; matrix products, arithmetic and copies ran while one was open for 1% of the time, Pallas kernels for 0%

profile of v1, /device:TPU:1, one launch (start us, length us, event | category | flops | bytes accessed | tf_op | source)
XLA Modules:
  0.0 223.5 jit_solution(4223417254324137005)
XLA Ops:
  0.0 0.0 copy-start.1
  0.0 2.5 %copy.61 = bf16[4,8,8,8192]{3,2,0,1:T(8,128)(2,1)S(1)} copy(bf16[4,8,8,8192]{3,2,1,0:T(8,128)(2,1)} %bitcast.100) | data formatting | bytes 8388608 | tf_op jit(solution)/shard_map/reshape | solution.py:85
  2.5 2.1 slice.94
  4.6 5.7 %collective-permute-start = (bf16[32,7,8192]{2,0,1:T(8,128)(2,1)}, bf16[32,7,8192]{2,0,1:T(8,128)(2,1)}, u32[]{:S(2)}, u32[]{:S(2)}) collective-permute-start(bf16[32,7,8192]{2,0,1:T(8,128)(2,1)} %slice.94), channel_id=1, source_target_pairs={{0,32},{32,64},{64,96},{96,128},{128,160},{160,192},{192,224},{1,3... | collective-permute-start | bytes 11010056 | tf_op jit(solution)/shard_map/ppermute | solution.py:14
  10.3 1.9 multiply_reduce_fusion
  13.0 0.0 copy-start
  13.0 0.0 copy-done.1
  13.0 1.2 broadcast_divide_fusion
  14.3 72.5 %collective-permute-done = bf16[32,7,8192]{2,0,1:T(8,128)(2,1)} collective-permute-done((bf16[32,7,8192]{2,0,1:T(8,128)(2,1)}, bf16[32,7,8192]{2,0,1:T(8,128)(2,1)}, u32[]{:S(2)}, u32[]{:S(2)}) %collective-permute-start) | collective-permute-done | bytes 3670048 | tf_op jit(solution)/shard_map/ppermute | solution.py:14
  86.8 2.3 %constant_dynamic-update-slice_fusion.1 = bf16[32,15,8192]{2,0,1:T(8,128)(2,1)S(1)} fusion(bf16[32,7,8192]{2,0,1:T(8,128)(2,1)} %collective-permute-done), kind=kLoop, calls=%fused_computation.99 | loop fusion | bytes 7340032
  89.1 0.0 copy-done
  89.1 0.4 constant_dynamic-update-slice_fusion
  89.6 7.9 %multiply_add_fusion = f32[32,8,8192]{2,0,1:T(8,128)S(1)} fusion(bf16[32,15,8192]{2,0,1:T(8,128)(2,1)S(1)} %constant_dynamic-update-slice_fusion, f32[8192]{0:T(1024)S(1)} %get-tuple-element.10, f32[8192]{0:T(1024)S(1)} %get-tuple-element.11, f32[8192]{0:T(1024)S(1)} %get-tuple-element.12, f32[8192]{0:T(1024)S(1)} %get-tuple-element.13, ...), kind=kLoop, calls=%fused_computation.12 | loop fusion | flops 48234496 | bytes 42205184 | tf_op jit(solution)/shard_map/add | solution.py:46
  97.5 38.5 %fusion.5 = f32[256,32,8]{0,1,2:T(8,128)S(1)} fusion(f32[32,8,8192]{2,0,1:T(8,128)S(1)} %multiply_add_fusion, s32[256]{0:T(256)S(1)} %iota_add_fusion.2), kind=kOutput, calls=%fused_computation.9 | convolution fusion | flops 6471811072 | bytes 8651776 | tf_op jit(solution)/shard_map/ifm,mk->kif/dot_general | solution.py:38
  135.9 38.8 %subtract_convert_fusion = (bf16[256,32,8]{0,1,2:T(8,128)(2,1)S(1)}, bf16[256,32,8]{0,1,2:T(8,128)(2,1)S(1)}) fusion(f32[256,32,8]{0,1,2:T(8,128)S(1)} %fusion.5, f32[256,32]{0,1:T(8,128)S(1)} %get-tuple-element.18, f32[256,32]{0,1:T(8,128)S(1)} %get-tuple-element.17, f32[32,8,8192]{2,0,1:T(8,128)S(1)} %multiply_add_fusion, s32[256]{0:T(256)S(1)} %iota_add_fusion.2), kind=kOutput, calls=%fused_computation.76 | convolution fusion | flops 6472400896 | bytes 8979456 | tf_op jit(solution)/shard_map/ifm,mk->kif/dot_general | solution.py:39
  174.8 0.3 copy.52
  175.1 0.3 copy.53
  175.8 1.0 reshape.152
  176.7 12.0 %all_to_all.14 = bf16[8,2,8192]{2,1,0:T(2,128)(2,1)S(1)} all-to-all(bf16[8,2,8192]{2,1,0:T(2,128)(2,1)S(1)} %reshape.152), channel_id=1, replica_groups=mesh['tm'=8,'stn'=32] {'tm'}, dimensions={0} | all-to-all | bytes 524288 | tf_op jit(solution)/shard_map/all_to_all | solution.py:68
  188.7 0.5 reshape.153
  189.2 0.3 copy_bitcast_fusion.1
  189.5 0.4 copy.51
  189.9 0.4 reshape.154
  190.2 26.8 %all_to_all.15 = bf16[32,2,2048]{2,1,0:T(2,128)(2,1)S(1)} all-to-all(bf16[32,2,2048]{2,1,0:T(2,128)(2,1)S(1)} %reshape.154), channel_id=1, replica_groups=mesh['tm'=8,'stn'=32] {'stn'}, dimensions={0} | all-to-all | bytes 524288 | tf_op jit(solution)/shard_map/all_to_all | solution.py:96
  217.0 0.4 reshape.155
  217.4 0.1 neg.22
  217.5 0.8 convolution_bitcast_fusion.1
  218.3 0.8 convolution_bitcast_fusion
  219.1 4.4 %maximum_multiply_fusion = f32[1,2,1024,1024]{3,2,1,0:T(8,128)} fusion(f32[1,1,1024,1024]{3,2,1,0:T(8,128)S(1)} %convolution_bitcast_fusion, f32[1,1,1024,1024]{3,2,1,0:T(8,128)S(1)} %convolution_bitcast_fusion.1), kind=kLoop, calls=%fused_computation.6 | loop fusion | flops 4194304 | bytes 16777216 | tf_op jit(solution)/shard_map/div | solution.py:61
  (12 shorter events, 0.4 us)
Async XLA Ops:
  0.0 13.0 %copy-start.1 = (f32[2,32,256]{2,1,0:T(8,128)S(1)}, f32[2,32,256]{2,1,0:T(8,128)}, u32[]{:S(2)}) copy-start(f32[2,32,256]{2,1,0:T(8,128)} %param.3) | copy-start | bytes 196612
  4.6 82.2 %collective-permute-start = (bf16[32,7,8192]{2,0,1:T(8,128)(2,1)}, bf16[32,7,8192]{2,0,1:T(8,128)(2,1)}, u32[]{:S(2)}, u32[]{:S(2)}) collective-permute-start(bf16[32,7,8192]{2,0,1:T(8,128)(2,1)} %slice.94), channel_id=1, source_target_pairs={{0,32},{32,64},{64,96},{96,128},{128,160},{160,192},{192,224},{1,3... | collective-permute-start | bytes 11010056 | tf_op jit(solution)/shard_map/ppermute | solution.py:14
  13.0 76.1 %copy-start = (bf16[32,65536]{1,0:T(8,128)(2,1)S(1)}, bf16[32,65536]{1,0:T(8,128)(2,1)}, u32[]{:S(2)}) copy-start(bf16[32,65536]{1,0:T(8,128)(2,1)} %param.2) | copy-start | bytes 12582916
